TPU v7x, 256 devices: a whole 4x4x8 slice. The times are simulated.
256 devices in a mesh: tok: 16 (over z, core), tp: 16 (over x, y).
Axes of the slice: x: 4, y: 4, z: 8, core: 2. Of those that a mesh axis runs over, the one named last changes fastest.
Arguments:
- hidden_states: bfloat16 [32768, 1024], P(('tok', 'tp')), may hold values from -40 to 40
- first_gain: float32 [1024], replicated, may hold values from 0.1 to 1.9
- second_gain: float32 [1024], replicated, may hold values from 0.1 to 1.9
- w_query: bfloat16 [1024, 1024], P(None, 'tp'), may hold values from -1 to 1
- w_keyval: bfloat16 [1024, 1024], replicated, may hold values from -0.375 to 0.375
- w_out: bfloat16 [1024, 1024], P('tp'), may hold values from -0.75 to 0.75
- kv_cache: bfloat16 [384, 128, 1024], P('tok'), may hold values from -310 to 310
- page_table: int32 [32, 16], P('tok'), may hold values from 0 to 383, as said below
- cached_len: int32 [32], P('tok'), may hold values from 128 to 2048, as said below
- expert_ids: int32 [32768, 8], P(('tok', 'tp')), may hold values from 0 to 31, all different within a row; in each aligned block of 128 rows (0 to 127, 128 to 255, ...) at most 64 rows name the same one
- gate_weights: float32 [32768, 8], P(('tok', 'tp')), may hold values from 0.1 to 1
- w_gate_up: bfloat16 [32, 1024, 1024], P('tp', 'tok'), may hold values from -0.1875 to 0.1875
- w_down: bfloat16 [32, 512, 1024], P('tp', 'tok'), may hold values from -1 to 1
Outputs:
- layer_out: bfloat16 [32768, 1024], P(('tok', 'tp'))
Inputs may be any that keep to these rules, and one draw needn't show every extreme that they name: `page_table`: request r's entries are pages of its own tok index, rows 24 * (r // 2) to 24 * (r // 2 + 1) - 1; its first 8 entries are the same for all requests of that tok index, and all other entries name pages that no other entry names. `cached_len`: some request has exactly 2048 cached tokens. `expert_ids`: in the rows of one device (aligned blocks of 128 rows) no expert is named by more than 64 rows, and a row names 8 different experts.
All inputs are finite; a program needn't handle non-finite values.
Results may differ from a plain program's by a relative error of at most 0.017.
The roundings to bfloat16 on the way count: a program that leaves them out, or rounds other values in their place, can miss the bound.
Values may be sent and summed in bfloat16 or wider, within the bound.
No kernel may reach another device: no remote copies, remote signals or barrier semaphores. Data moves between devices by JAX's collectives and lax.ppermute only.
A program may use at most 128 MiB of HBM per device.

v0:
```python
import jax
import jax.numpy as jnp
from jax import lax
from jax.sharding import Mesh
from jax.sharding import PartitionSpec as P

D = 1024
HEADS = 16
KV_HEADS = 8
HEAD_DIM = 64
EXPERTS = 32
FF_EXPERT = 512
TOP = 8
NEW = 1024
MAX_CACHED = 2048
REQ_DEV = 2
ATTN_SCALE = 0.015625
EPSILON = 1e-06
THETA = 10000.0
TOK = ("tz", "tc")
TP = ("ra", "rb")


def rms_norm(values, gain):
    wide = values.astype(jnp.float32)
    factor = lax.rsqrt(jnp.mean(wide * wide, axis=-1, keepdims=True) + EPSILON)
    return (wide * factor * gain).astype(jnp.bfloat16)


def rotate(values, positions):
    row_count = values.shape[0]
    shaped = values.reshape(row_count, -1, HEAD_DIM)
    half_dim = HEAD_DIM // 2
    exponent = jnp.arange(half_dim).astype(jnp.float32) * (2.0 / HEAD_DIM)
    frequency = jnp.power(THETA, -exponent)
    angles = positions.astype(jnp.float32)[:, None] * frequency[None, :]
    cosine = jnp.cos(angles)[:, None, :]
    sine_part = jnp.sin(angles)[:, None, :]
    leading = shaped[..., :half_dim]
    trailing = shaped[..., half_dim:]
    turned = jnp.concatenate(
        [leading * cosine - trailing * sine_part, trailing * cosine + leading * sine_part], axis=-1
    )
    return turned.reshape(row_count, -1)


def shards(
    hidden_states,
    first_gain,
    second_gain,
    w_query,
    w_keyval,
    w_out,
    kv_cache,
    page_table,
    cached_len,
    expert_ids,
    gate_weights,
    w_gate_up,
    w_down,
):
    tok_rows = hidden_states.shape[0]
    tp_size = lax.axis_size(TP)
    core = lax.axis_index("tc")
    local_req = lax.axis_index("ra")
    block = lax.axis_index("rb")
    kv_cols = KV_HEADS * HEAD_DIM
    group_size = HEADS // KV_HEADS
    half_rows = D // 2
    wq_half = lax.dynamic_slice_in_dim(w_query, core * half_rows, half_rows, 0)
    wq_full = lax.all_gather(
        lax.all_gather(wq_half, TP, axis=1, tiled=True), "tc", axis=0, tiled=True
    )
    wo_half = lax.dynamic_slice_in_dim(w_out, core * half_rows, half_rows, 1)
    wo_full = lax.all_gather(
        lax.all_gather(wo_half, TP, axis=0, tiled=True), "tc", axis=1, tiled=True
    )
    gate_up_full = lax.all_gather(w_gate_up, TOK, axis=1, tiled=True)
    down_full = lax.all_gather(w_down, TOK, axis=1, tiled=True)
    normed = rms_norm(hidden_states, first_gain)
    length = cached_len[local_req]
    positions = length + block * tok_rows + jnp.arange(tok_rows, dtype=jnp.int32)
    keyval = jnp.dot(normed, w_keyval, preferred_element_type=jnp.float32)
    new_kv = jnp.concatenate(
        [rotate(keyval[:, :kv_cols], positions), keyval[:, kv_cols:]], axis=1
    ).astype(jnp.bfloat16)
    request_kv = lax.all_gather(new_kv, "rb", axis=0, tiled=True)
    queries = rotate(
        jnp.dot(normed, wq_full, preferred_element_type=jnp.float32), positions
    ).astype(jnp.bfloat16)
    local_pages = page_table[local_req] - lax.axis_index(TOK) * kv_cache.shape[0]
    cached = jnp.take(kv_cache, local_pages, axis=0).reshape(MAX_CACHED, 2 * kv_cols)
    keys_total = jnp.concatenate([cached[:, :kv_cols], request_kv[:, :kv_cols]], axis=0).reshape(
        MAX_CACHED + NEW, KV_HEADS, HEAD_DIM
    )
    values_total = jnp.concatenate([cached[:, kv_cols:], request_kv[:, kv_cols:]], axis=0).reshape(
        MAX_CACHED + NEW, KV_HEADS, HEAD_DIM
    )
    grouped_q = queries.reshape(tok_rows, KV_HEADS, group_size, HEAD_DIM)
    scores = (
        jnp.einsum("qgpd,kgd->gpqk", grouped_q, keys_total, preferred_element_type=jnp.float32)
        * ATTN_SCALE
    )
    key_index = jnp.arange(MAX_CACHED + NEW, dtype=jnp.int32)
    query_pos = block * tok_rows + jnp.arange(tok_rows, dtype=jnp.int32)
    allowed = jnp.where(
        key_index[None, :] < MAX_CACHED,
        key_index[None, :] < length,
        key_index[None, :] - MAX_CACHED <= query_pos[:, None],
    )
    scores = jnp.where(allowed, scores, -1e30)
    top_score = jnp.max(scores, axis=-1, keepdims=True)
    weights = jnp.exp(scores - top_score)
    probs = (weights / jnp.sum(weights, axis=-1, keepdims=True)).astype(jnp.bfloat16)
    attended = (
        jnp.einsum("gpqk,kgd->qgpd", probs, values_total, preferred_element_type=jnp.float32)
        .astype(jnp.bfloat16)
        .reshape(tok_rows, HEADS * HEAD_DIM)
    )
    projected_out = jnp.dot(attended, wo_full, preferred_element_type=jnp.float32)
    middle = (hidden_states.astype(jnp.float32) + projected_out).astype(jnp.bfloat16)
    normed_two = rms_norm(middle, second_gain)
    experts_local = EXPERTS // tp_size
    capacity = 2 * tok_rows * TOP // EXPERTS
    expert_range = jnp.arange(EXPERTS, dtype=jnp.int32)
    onehot = (expert_ids[:, :, None] == expert_range[None, None, :]).astype(jnp.int32)
    per_token = jnp.sum(onehot, axis=1)
    earlier = jnp.cumsum(per_token, axis=0) - per_token
    slot_ids = jnp.sum(onehot * earlier[:, None, :], axis=2)
    target = expert_ids * capacity + slot_ids
    outgoing_rows = jnp.broadcast_to(normed_two[:, None, :], (tok_rows, TOP, D))
    send_buffer = jnp.zeros((EXPERTS * capacity, D), jnp.bfloat16).at[target].set(outgoing_rows)
    received = lax.all_to_all(
        send_buffer.reshape(tp_size, experts_local, capacity, D),
        TP,
        split_axis=0,
        concat_axis=2,
        tiled=True,
    )
    received = received.reshape(experts_local, tp_size * capacity, D)
    both = jnp.einsum("esd,edf->esf", received, gate_up_full, preferred_element_type=jnp.float32)
    activated = (jax.nn.silu(both[..., :FF_EXPERT]) * both[..., FF_EXPERT:]).astype(jnp.bfloat16)
    produced = jnp.einsum(
        "esf,efd->esd", activated, down_full, preferred_element_type=jnp.float32
    ).astype(jnp.bfloat16)
    returned = lax.all_to_all(
        produced.reshape(experts_local, tp_size, capacity, D),
        TP,
        split_axis=1,
        concat_axis=0,
        tiled=True,
    )
    returned = returned.reshape(EXPERTS * capacity, D)
    picked = returned[target]
    mixture = jnp.einsum("tk,tkd->td", gate_weights, picked.astype(jnp.float32))
    return (middle.astype(jnp.float32) + mixture).astype(jnp.bfloat16)


def solution(mesh):
    tok_size, tp_size = mesh.devices.shape
    group = tp_size // REQ_DEV
    split = Mesh(mesh.devices.reshape(tok_size // 2, 2, REQ_DEV, group), TOK + TP)
    in_specs = (
        P(TOK + TP, None),
        P(),
        P(),
        P(None, TP),
        P(),
        P(TP, None),
        P(TOK, None, None),
        P(TOK, None),
        P(TOK),
        P(TOK + TP, None),
        P(TOK + TP, None),
        P(TP, TOK, None),
        P(TP, TOK, None),
    )
    out_specs = P(TOK + TP, None)
    return jax.shard_map(
        shards, mesh=split, in_specs=in_specs, out_specs=out_specs, check_vma=False
    )
```

profile of v0, /device:TPU:28, one launch (start us, length us, event | category | flops | bytes accessed | tf_op | source)
XLA Modules:
  0.0 387.6 jit_solution(11292400467645476767)
XLA Ops:
  6.5 1.6 constant_dynamic-slice_fusion.1
  8.2 1.5 constant_dynamic-slice_fusion
  9.8 1.1 fusion.20
  10.9 1.4 fusion.26
  14.9 43.1 %all-gather.10.cloned.1.call-done = bf16[512,1024]{0,1:T(8,128)(2,1)} async-done(((bf16[512,64]{0,1:T(8,128)(2,1)}), bf16[512,1024]{0,1:T(8,128)(2,1)}) %all-gather.10.cloned.1.call-update) | async-done | bytes 1048592 | tf_op jit(solution)/shard_map/all_gather | solution.py:72
  58.1 49.3 %all-gather.14.cloned.1.call-done = bf16[1024,512]{1,0:T(8,128)(2,1)} async-done(((bf16[64,512]{1,0:T(8,128)(2,1)}), bf16[1024,512]{1,0:T(8,128)(2,1)}) %all-gather.14.cloned.1.call-update) | async-done | bytes 1048592 | tf_op jit(solution)/shard_map/all_gather | solution.py:76
  108.7 5.5 %gather_fusion = bf16[16,128,1024]{2,1,0:T(8,128)(2,1)} fusion(bf16[24,128,1024]{2,1,0:T(8,128)(2,1)} %param.19, s32[1024]{0:T(1024)S(1)} %pad_clamp_fusion), kind=kCustom, calls=%fused_computation | custom fusion | bytes 8388672 | tf_op jit(solution)/shard_map/jit(_take)/gather | solution.py:92
  114.3 6.6 %copy.43 = bf16[2048,1024]{0,1:T(8,128)(2,1)} copy(bf16[2048,1024]{1,0:T(8,128)(2,1)} %bitcast.74) | data formatting | bytes 8388608 | tf_op jit(solution)/shard_map/jit(_take)/gather | solution.py:92
  120.9 2.7 broadcast_select_fusion
  123.6 1.6 fusion.33
  125.7 3.5 compare_select_fusion
  129.4 22.4 %all-gather.8.cloned.1.call-done = bf16[1024,1024]{1,0:T(8,128)(2,1)} async-done(((bf16[128,1024]{1,0:T(8,128)(2,1)}), bf16[1024,1024]{1,0:T(8,128)(2,1)}) %all-gather.8.cloned.1.call-update) | async-done | bytes 2097168 | tf_op jit(solution)/shard_map/all_gather | solution.py:87
  151.9 3.0 fusion.34
  154.8 1.5 copy.46
  156.3 2.3 copy.47
  158.6 4.3 %pad_maximum_fusion = (bf16[3072,512]{0,1:T(8,128)(2,1)}, bf16[3072,512]{0,1:T(8,128)(2,1)}) fusion(bf16[1024,512]{0,1:T(8,128)(2,1)S(1)} %copy.46, bf16[2048,512]{0,1:T(8,128)(2,1)} %get-tuple-element.6, bf16[1024,512]{0,1:T(8,128)(2,1)} %copy.47, bf16[2048,512]{0,1:T(8,128)(2,1)S(1)} %get-tuple-element.5), kind=kLoop, calls=%fused_computation.15 | loop fusion | flops 12582912 | bytes 12582912 | tf_op jit(solution)/shard_map/concatenate | solution.py:96
  162.9 8.4 %all-gather.12.cloned.1.call-done = bf16[1024,1024]{0,1:T(8,128)(2,1)} async-done(((bf16[512,1024]{0,1:T(8,128)(2,1)}), bf16[1024,1024]{0,1:T(8,128)(2,1)}) %all-gather.12.cloned.1.call-update) | async-done | bytes 2097168 | tf_op jit(solution)/shard_map/all_gather | solution.py:71
  171.3 2.4 fusion.24
  173.8 14.0 %fusion.35 = (f32[8,2,128]{2,1,0:T(2,128)S(1)}, f32[8,2,128,3072]{2,3,1,0:T(8,128)}) fusion(pred[128,3072]{0,1:T(8,128)(4,1)S(1)} %copy-done.3, bf16[3072,8,64,1]{0,2,3,1:T(8,128)(2,1)} %bitcast.78, bf16[128,8,2,64]{0,3,2,1:T(8,128)(2,1)S(1)} %bitcast.82), kind=kOutput, calls=%fused_computation.80 | convolution fusion | flops 830475264 | bytes 28975104 | tf_op jit(solution)/shard_map/sub | solution.py:113
  187.8 11.7 %fusion.18 = bf16[8,64,2,128]{3,1,2,0:T(8,128)(2,1)S(1)} fusion(bf16[3072,8,64,1]{0,2,3,1:T(8,128)(2,1)} %bitcast.77, f32[8,2,128,3072]{2,3,1,0:T(8,128)} %get-tuple-element.16, f32[8,2,128]{2,1,0:T(2,128)S(1)} %get-tuple-element.15), kind=kOutput, calls=%fused_computation.29 | convolution fusion | flops 818020352 | bytes 28581888 | tf_op jit(solution)/shard_map/gpqk,kgd->qgpd/dot_general | solution.py:116
  199.6 2.1 multiply_reduce_fusion
  201.8 8.1 %scatter_custom_fusion = bf16[2048,1024]{1,0:T(8,128)(2,1)} fusion(s32[1024]{0:T(1024)S(1)} %reshape.206, bf16[]{:T(256)} %constant.75.clone.1, bf16[128,1024]{1,0:T(8,128)(2,1)S(1)} %multiply_convert_fusion), kind=kCustom, calls=%fused_computation.21 | custom fusion | bytes 4456450 | tf_op jit(solution)/shard_map/scatter | solution.py:132
  210.0 7.2 %all-to-all-start = ((bf16[16,2,64,1024]{3,2,1,0:T(8,128)(2,1)}), bf16[16,2,64,1024]{3,2,1,0:T(8,128)(2,1)}, u32[]{:S(2)}, u32[]{:S(2)}) async-start(bf16[16,2,64,1024]{3,2,1,0:T(8,128)(2,1)} %bitcast.73), calls=%async_computation | async-start | bytes 8388608 | tf_op jit(solution)/shard_map/all_to_all | solution.py:133
  217.9 61.8 %all-to-all-done = bf16[16,2,64,1024]{3,2,1,0:T(8,128)(2,1)} async-done(((bf16[16,2,64,1024]{3,2,1,0:T(8,128)(2,1)}), bf16[16,2,64,1024]{3,2,1,0:T(8,128)(2,1)}, u32[]{:S(2)}, u32[]{:S(2)}) %all-to-all-start) | async-done | bytes 4194336 | tf_op jit(solution)/shard_map/all_to_all | solution.py:133
  279.7 4.9 %copy.54 = bf16[1,2,16,64,1024]{4,3,2,1,0:T(8,128)(2,1)} copy(bf16[1,2,16,64,1024]{4,3,1,2,0:T(8,128)(2,1)} %bitcast.22) | data formatting | bytes 8388608 | tf_op jit(solution)/shard_map/all_to_all | solution.py:133
  284.6 11.2 %fusion.36 = f32[2,1024,1024]{2,1,0:T(8,128)} fusion(bf16[2,1024,1024]{2,1,0:T(8,128)(2,1)} %bitcast.75, bf16[2,1024,1024]{2,1,0:T(8,128)(2,1)} %all-gather.18.cloned.1.call-done), kind=kOutput, calls=%fused_computation.81 | convolution fusion | flops 4294967296 | bytes 16777216 | tf_op jit(solution)/shard_map/esd,edf->esf/dot_general | solution.py:141
  295.8 6.4 %convolution_convert_fusion = bf16[2,1024,1024]{2,1,0:T(8,128)(2,1)S(1)} fusion(bf16[2,512,1024]{2,1,0:T(8,128)(2,1)} %all-gather.20.cloned.1.call-done, f32[2,1024,1024]{2,1,0:T(8,128)} %fusion.36), kind=kOutput, calls=%fused_computation.18 | convolution fusion | flops 2155872256 | bytes 14680064 | tf_op jit(solution)/shard_map/esf,efd->esd/dot_general | solution.py:143
  302.2 2.5 copy.55
  304.7 7.9 %all-to-all-start.1 = ((bf16[2,16,64,1024]{3,2,0,1:T(8,128)(2,1)}), bf16[2,16,64,1024]{3,2,0,1:T(8,128)(2,1)}, u32[]{:S(2)}, u32[]{:S(2)}) async-start(bf16[2,16,64,1024]{3,2,0,1:T(8,128)(2,1)} %copy.55), calls=%async_computation.1 | async-start | bytes 8388608 | tf_op jit(solution)/shard_map/all_to_all | solution.py:146
  312.7 56.0 %all-to-all-done.1 = bf16[2,16,64,1024]{3,2,0,1:T(8,128)(2,1)} async-done(((bf16[2,16,64,1024]{3,2,0,1:T(8,128)(2,1)}), bf16[2,16,64,1024]{3,2,0,1:T(8,128)(2,1)}, u32[]{:S(2)}, u32[]{:S(2)}) %all-to-all-start.1) | async-done | bytes 4194336 | tf_op jit(solution)/shard_map/all_to_all | solution.py:146
  368.8 8.9 %gather_fusion.1 = bf16[1024,1024]{1,0:T(8,128)(2,1)} fusion(bf16[2048,1024]{1,0:T(8,128)(2,1)} %bitcast.27, s32[1024]{0:T(1024)S(1)} %broadcast_clamp_fusion), kind=kCustom, calls=%fused_computation.1 | custom fusion | bytes 4198400 | tf_op jit(solution)/shard_map/gather | solution.py:154
  377.7 2.3 fusion.10
  (72 shorter events, 6.0 us)
Async XLA Ops:
  6.5 4.3 %copy-start = (bf16[1024,1024]{1,0:T(8,128)(2,1)S(1)}, bf16[1024,1024]{1,0:T(8,128)(2,1)}, u32[]{:S(2)}) copy-start(bf16[1024,1024]{1,0:T(8,128)(2,1)} %param.17) | copy-start | bytes 6291460
  6.5 6.0 %copy-start.9 = (s32[2]{0:T(128)S(1)}, s32[2]{0:T(128)}, u32[]{:S(2)}) copy-start(s32[2]{0:T(128)} %param.21) | copy-start | bytes 28
  6.5 51.5 %all-gather.10.cloned.1.call-start = ((), (), s32[]{:S(2)}) async-start(), calls=%async_computation.3 | async-start | bytes 1114112 | tf_op jit(solution)/shard_map/all_gather | solution.py:72
  8.2 99.2 %all-gather.14.cloned.1.call-start = ((), (), s32[]{:S(2)}) async-start(), calls=%async_computation.5 | async-start | bytes 1114112 | tf_op jit(solution)/shard_map/all_gather | solution.py:76
  9.7 142.1 %all-gather.8.cloned.1.call-start = ((), (), s32[]{:S(2)}) async-start(), calls=%async_computation.2 | async-start | bytes 2359296 | tf_op jit(solution)/shard_map/all_gather | solution.py:87
  10.9 97.1 %copy-start.8 = (s32[2,16]{1,0:T(2,128)S(1)}, s32[2,16]{1,0:T(2,128)}, u32[]{:S(2)}) copy-start(s32[2,16]{1,0:T(2,128)} %param.20) | copy-start | bytes 388
  14.9 156.4 %all-gather.12.cloned.1.call-start = ((), (), s32[]{:S(2)}) async-start(), calls=%async_computation.4 | async-start | bytes 3145728 | tf_op jit(solution)/shard_map/all_gather | solution.py:71
  58.1 141.5 %all-gather.16.cloned.1.call-start = ((), (), s32[]{:S(2)}) async-start(), calls=%async_computation.6 | async-start | bytes 3145728 | tf_op jit(solution)/shard_map/all_gather | solution.py:75
  107.4 177.1 %all-gather.18.cloned.1.call-start = ((), (), s32[]{:S(2)}) async-start(), calls=%async_computation.7 | async-start | bytes 4456448 | tf_op jit(solution)/shard_map/all_gather | solution.py:78
  123.6 1.7 copy-start.4
  158.6 12.7 %copy-start.2 = (bf16[128,1024]{1,0:T(8,128)(2,1)S(1)}, bf16[128,1024]{1,0:T(8,128)(2,1)}, u32[]{:S(2)}) copy-start(bf16[128,1024]{1,0:T(8,128)(2,1)} %param.13) | copy-start | bytes 786436
  158.6 12.7 %copy-start.5 = (f32[1024]{0:T(1024)S(1)}, f32[1024]{0:T(1024)}, u32[]{:S(2)}) copy-start(f32[1024]{0:T(1024)} %param.14) | copy-start | bytes 12292
  162.9 10.9 %copy-start.3 = (pred[128,3072]{0,1:T(8,128)(4,1)S(1)}, pred[128,3072]{0,1:T(8,128)(4,1)}, u32[]{:S(2)}) copy-start(pred[128,3072]{0,1:T(8,128)(4,1)} %compare_select_fusion) | copy-start | bytes 1179652
  187.8 13.9 %copy-start.6 = (f32[1024]{0:T(1024)S(1)}, f32[1024]{0:T(1024)}, u32[]{:S(2)}) copy-start(f32[1024]{0:T(1024)} %param.15) | copy-start | bytes 12292
  210.0 69.7 %all-to-all-start = ((bf16[16,2,64,1024]{3,2,1,0:T(8,128)(2,1)}), bf16[16,2,64,1024]{3,2,1,0:T(8,128)(2,1)}, u32[]{:S(2)}, u32[]{:S(2)}) async-start(bf16[16,2,64,1024]{3,2,1,0:T(8,128)(2,1)} %bitcast.73), calls=%async_computation | async-start | bytes 8388608 | tf_op jit(solution)/shard_map/all_to_all | solution.py:133
  217.2 78.6 %all-gather.20.cloned.1.call-start = ((), (), s32[]{:S(2)}) async-start(), calls=%async_computation.8 | async-start | bytes 2228224 | tf_op jit(solution)/shard_map/all_gather | solution.py:79
  304.7 7.9 %copy-start.7 = (f32[128,8]{0,1:T(8,128)S(1)}, f32[128,8]{0,1:T(8,128)}, u32[]{:S(2)}) copy-start(f32[128,8]{0,1:T(8,128)} %param.23) | copy-start | bytes 12292
  304.7 64.1 %all-to-all-start.1 = ((bf16[2,16,64,1024]{3,2,0,1:T(8,128)(2,1)}), bf16[2,16,64,1024]{3,2,0,1:T(8,128)(2,1)}, u32[]{:S(2)}, u32[]{:S(2)}) async-start(bf16[2,16,64,1024]{3,2,0,1:T(8,128)(2,1)} %copy.55), calls=%async_computation.1 | async-start | bytes 8388608 | tf_op jit(solution)/shard_map/all_to_all | solution.py:146
  368.8 12.0 %copy-start.1 = (bf16[1024,1024]{1,0:T(8,128)(2,1)S(1)}, bf16[1024,1024]{1,0:T(8,128)(2,1)}, u32[]{:S(2)}) copy-start(bf16[1024,1024]{1,0:T(8,128)(2,1)} %param.17) | copy-start | bytes 6291460
Sparse Core Ops, SparseCore 0:
  9.8 48.2 all-gather.9
  60.5 46.8 all-gather.13
  109.2 42.6 all-gather.7
  153.5 17.7 all-gather.11
  172.9 17.1 all-gather.15
  191.9 43.1 all-gather.17
  236.9 38.0 all-gather.19
where the time goes:
time: 388 us
  waiting for transfers between devices  242 us (62%)
  matrix products  51.6 us (13%)
  local copies, waits for them, and re-layouts  49.4 us (13%)
  starting transfers between devices  15.3 us (4%)
  other arithmetic  14.5 us (4%)
  between operations  14.4 us (4%)
    all_to_all x1, waiting for transfers between devices, shards(): lax.all_to_all(send_buffer.reshape(tp_size, experts_local, capacity, D),...  61.8 us
    all_to_all x1, waiting for transfers between devices, shards(): lax.all_to_all(produced.reshape(experts_local, tp_size, capacity, D), TP,...  56 us
    all_gather x1, waiting for transfers between devices, shards(): lax.all_gather(wo_half, TP, axis=0, tiled=True)  49.3 us
    all_gather x1, waiting for transfers between devices, shards(): lax.all_gather(wq_half, TP, axis=1, tiled=True)  43.1 us
    all_gather x1, waiting for transfers between devices, shards(): request_kv = lax.all_gather(new_kv, 'rb', axis=0, tiled=True)  22.4 us
    sub x1, matrix products, shards(): weights = jnp.exp(scores - top_score)  14 us
    gather x2, local copies, waits for them, and re-layouts, shards(): jnp.take(kv_cache, local_pages, axis=0).reshape(MAX_CACHED, 2 * kv_cols)  12.1 us
    dot_general x1, matrix products, shards(): jnp.einsum('gpqk,kgd->qgpd', probs, values_total, preferred_element_type=...  11.7 us
  transfers between devices with their start and end apart: 9, of which 6 were waited for; matrix products, arithmetic and copies ran while one was open for 24% of the time, Pallas kernels for 0%

commit v1 on v0

--- a/solution.py
+++ b/solution.py
@@ -19,6 +19,13 @@
 THETA = 10000.0
 TOK = ("tz", "tc")
 TP = ("ra", "rb")
+
+
+def gather_over(x, name, dim):
+    size = lax.axis_size(name)
+    tiles = jnp.stack([x for _ in range(size)])
+    tiles = lax.all_to_all(tiles, name, split_axis=0, concat_axis=0)
+    return jnp.concatenate(tiles, axis=dim)
 
 
 def rms_norm(values, gain):
@@ -68,9 +75,7 @@
     group_size = HEADS // KV_HEADS
     half_rows = D // 2
     wq_half = lax.dynamic_slice_in_dim(w_query, core * half_rows, half_rows, 0)
-    wq_full = lax.all_gather(
-        lax.all_gather(wq_half, TP, axis=1, tiled=True), "tc", axis=0, tiled=True
-    )
+    wq_full = gather_over(lax.all_gather(wq_half, TP, axis=1, tiled=True), "tc", 0)
     wo_half = lax.dynamic_slice_in_dim(w_out, core * half_rows, half_rows, 1)
     wo_full = lax.all_gather(
         lax.all_gather(wo_half, TP, axis=0, tiled=True), "tc", axis=1, tiled=True

time: 388 us -> 361 us (0.930)
  waiting for transfers between devices: 242 us -> 202 us
  blocking collectives: 0 us -> 6.45 us
  local copies, waits for them, and re-layouts: 49.4 us -> 54.3 us
    all_gather x1, waiting for transfers between devices: 43.1 us -> 26.7 us  [shards(): lax.all_gather(wq_half, TP, axis=1, tiled=True)]
    all_to_all x1, waiting for transfers between devices: 61.8 us -> 48.2 us  [shards(): lax.all_to_all(send_buffer.reshape(tp_size, experts_local, capacity, D),...]
    all_gather x1, waiting for transfers between devices: 22.4 us -> 31.8 us  [shards(): request_kv = lax.all_gather(new_kv, 'rb', axis=0, tiled=True)]
    all_gather x1 -> x0, waiting for transfers between devices: 8.38 us -> none  [shards(): lax.all_gather(lax.all_gather(wq_half, TP, axis=1, tiled=True), 'tc', axi...]
    all_to_all x0 -> x1, blocking collectives: none -> 6.45 us  [gather_over(): tiles = lax.all_to_all(tiles, name, split_axis=0, concat_axis=0)]
    all_gather x1, waiting for transfers between devices: 49.3 us -> 43 us  [shards(): lax.all_gather(wo_half, TP, axis=0, tiled=True)]
    all_to_all x1, waiting for transfers between devices: 56 us -> 51.6 us  [shards(): lax.all_to_all(produced.reshape(experts_local, tp_size, capacity, D), TP,...]
  transfers between devices with their start and end apart: 9 -> 8, of which waited for: 6 -> 5; matrix products, arithmetic and copies ran while one was open for 24% -> 27% of each run, Pallas kernels for 0% -> 0%
where the time goes in v1:
time: 361 us; the launch traced here: 358 us
  waiting for transfers between devices  202 us (56%)
  local copies, waits for them, and re-layouts  54.3 us (15%)
  matrix products  49.8 us (14%)
  other arithmetic  15.4 us (4%)
  starting transfers between devices  15.1 us (4%)
  between operations  14.5 us (4%)
  blocking collectives  6.45 us (2%)
    all_to_all x1, waiting for transfers between devices, shards(): lax.all_to_all(produced.reshape(experts_local, tp_size, capacity, D), TP,...  51.6 us
    all_to_all x1, waiting for transfers between devices, shards(): lax.all_to_all(send_buffer.reshape(tp_size, experts_local, capacity, D),...  48.2 us
    all_gather x1, waiting for transfers between devices, shards(): lax.all_gather(wo_half, TP, axis=0, tiled=True)  43 us
    all_gather x1, waiting for transfers between devices, shards(): request_kv = lax.all_gather(new_kv, 'rb', axis=0, tiled=True)  31.8 us
    all_gather x1, waiting for transfers between devices, shards(): lax.all_gather(wq_half, TP, axis=1, tiled=True)  26.7 us
    sub x1, matrix products, shards(): weights = jnp.exp(scores - top_score)  14 us
    gather x2, local copies, waits for them, and re-layouts, shards(): jnp.take(kv_cache, local_pages, axis=0).reshape(MAX_CACHED, 2 * kv_cols)  12.1 us
    dot_general x1, matrix products, shards(): jnp.einsum('gpqk,kgd->qgpd', probs, values_total, preferred_element_type=...  11.5 us
  transfers between devices with their start and end apart: 8, of which 5 were waited for; matrix products, arithmetic and copies ran while one was open for 27% of the time, Pallas kernels for 0%

profile of v1, /device:TPU:28, one launch (start us, length us, event | category | flops | bytes accessed | tf_op | source)
XLA Modules:
  0.0 357.9 jit_solution(3078815719426229397)
XLA Ops:
  6.6 1.6 constant_dynamic-slice_fusion
  8.2 1.5 constant_dynamic-slice_fusion.1
  10.9 1.4 fusion.27
  15.1 43.0 %all-gather.11.cloned.1.call-done = bf16[1024,512]{1,0:T(8,128)(2,1)} async-done(((bf16[64,512]{1,0:T(8,128)(2,1)}), bf16[1024,512]{1,0:T(8,128)(2,1)}) %all-gather.11.cloned.1.call-update) | async-done | bytes 1048592 | tf_op jit(solution)/shard_map/all_gather | solution.py:81
  59.5 5.6 %gather_fusion = bf16[16,128,1024]{2,1,0:T(8,128)(2,1)} fusion(bf16[24,128,1024]{2,1,0:T(8,128)(2,1)} %param.19, s32[1024]{0:T(1024)S(1)} %pad_clamp_fusion), kind=kCustom, calls=%fused_computation | custom fusion | bytes 8388672 | tf_op jit(solution)/shard_map/jit(_take)/gather | solution.py:97
  65.0 6.6 %copy.46 = bf16[2048,1024]{0,1:T(8,128)(2,1)} copy(bf16[2048,1024]{1,0:T(8,128)(2,1)} %bitcast.81) | data formatting | bytes 8388608 | tf_op jit(solution)/shard_map/jit(_take)/gather | solution.py:97
  71.6 2.6 broadcast_select_fusion
  74.3 2.3 fusion.34
  77.2 3.6 compare_select_fusion
  80.7 26.7 %all-gather.9.cloned.1.call-done = bf16[512,1024]{0,1:T(8,128)(2,1)} async-done(((bf16[512,64]{0,1:T(8,128)(2,1)}), bf16[512,1024]{0,1:T(8,128)(2,1)}) %all-gather.9.cloned.1.call-update) | async-done | bytes 1048592 | tf_op jit(solution)/shard_map/all_gather | solution.py:78
  107.4 1.5 copy.51
  109.1 6.5 %all_to_all.35 = bf16[2,512,1024]{2,1,0:T(8,128)(2,1)} all-to-all(bf16[2,512,1024]{2,1,0:T(8,128)(2,1)S(1)} %pad_maximum_fusion.2), channel_id=1, replica_groups=mesh['tz'=8,'tc'=2,'ra'=2,'rb'=8] {'tc'}, dimensions={0} | all-to-all | bytes 4194304 | tf_op jit(solution)/shard_map/all_to_all | solution.py:27
  115.6 2.9 copy.52
  120.1 31.8 %all-gather.7.cloned.1.call-done = bf16[1024,1024]{1,0:T(8,128)(2,1)} async-done(((bf16[128,1024]{1,0:T(8,128)(2,1)}), bf16[1024,1024]{1,0:T(8,128)(2,1)}) %all-gather.7.cloned.1.call-update) | async-done | bytes 2097168 | tf_op jit(solution)/shard_map/all_gather | solution.py:92
  151.9 3.0 fusion.35
  154.8 1.5 copy.49
  156.3 2.3 copy.50
  158.6 4.3 %pad_maximum_fusion = (bf16[3072,512]{0,1:T(8,128)(2,1)}, bf16[3072,512]{0,1:T(8,128)(2,1)}) fusion(bf16[1024,512]{0,1:T(8,128)(2,1)S(1)} %copy.49, bf16[2048,512]{0,1:T(8,128)(2,1)} %get-tuple-element.6, bf16[1024,512]{0,1:T(8,128)(2,1)} %copy.50, bf16[2048,512]{0,1:T(8,128)(2,1)S(1)} %copy-done.2), kind=kLoop, calls=%fused_computation.15 | loop fusion | flops 12582912 | bytes 12582912 | tf_op jit(solution)/shard_map/concatenate | solution.py:101
  162.9 14.0 %fusion.36 = (f32[8,2,128]{2,1,0:T(2,128)S(1)}, f32[8,2,128,3072]{2,3,1,0:T(8,128)}) fusion(pred[128,3072]{0,1:T(8,128)(4,1)} %compare_select_fusion, bf16[3072,8,64,1]{0,2,3,1:T(8,128)(2,1)} %bitcast.88, bf16[128,8,2,64]{0,3,2,1:T(8,128)(2,1)} %bitcast.91), kind=kOutput, calls=%fused_computation.82 | convolution fusion | flops 830475264 | bytes 28975104 | tf_op jit(solution)/shard_map/sub | solution.py:118
  176.8 11.5 %fusion.18 = bf16[8,64,2,128]{3,1,2,0:T(8,128)(2,1)S(1)} fusion(bf16[3072,8,64,1]{0,2,3,1:T(8,128)(2,1)} %bitcast.87, f32[8,2,128,3072]{2,3,1,0:T(8,128)} %get-tuple-element.16, f32[8,2,128]{2,1,0:T(2,128)S(1)} %get-tuple-element.15), kind=kOutput, calls=%fused_computation.30 | convolution fusion | flops 818020352 | bytes 28581888 | tf_op jit(solution)/shard_map/gpqk,kgd->qgpd/dot_general | solution.py:121
  188.4 2.1 multiply_reduce_fusion
  190.7 7.9 %scatter_custom_fusion = bf16[2048,1024]{1,0:T(8,128)(2,1)} fusion(s32[1024]{0:T(1024)S(1)} %reshape.208, bf16[]{:T(256)} %constant.75.clone.1, bf16[128,1024]{1,0:T(8,128)(2,1)S(1)} %multiply_convert_fusion), kind=kCustom, calls=%fused_computation.22 | custom fusion | bytes 4456450 | tf_op jit(solution)/shard_map/scatter | solution.py:137
  198.6 7.8 %all-to-all-start.1 = ((bf16[16,2,64,1024]{3,2,1,0:T(8,128)(2,1)}), bf16[16,2,64,1024]{3,2,1,0:T(8,128)(2,1)}, u32[]{:S(2)}, u32[]{:S(2)}) async-start(bf16[16,2,64,1024]{3,2,1,0:T(8,128)(2,1)} %bitcast.80), calls=%async_computation.1 | async-start | bytes 8388608 | tf_op jit(solution)/shard_map/all_to_all | solution.py:138
  207.0 48.2 %all-to-all-done.1 = bf16[16,2,64,1024]{3,2,1,0:T(8,128)(2,1)} async-done(((bf16[16,2,64,1024]{3,2,1,0:T(8,128)(2,1)}), bf16[16,2,64,1024]{3,2,1,0:T(8,128)(2,1)}, u32[]{:S(2)}, u32[]{:S(2)}) %all-to-all-start.1) | async-done | bytes 4194336 | tf_op jit(solution)/shard_map/all_to_all | solution.py:138
  255.2 4.9 %copy.58 = bf16[1,2,16,64,1024]{4,3,2,1,0:T(8,128)(2,1)} copy(bf16[1,2,16,64,1024]{4,3,1,2,0:T(8,128)(2,1)} %bitcast.26) | data formatting | bytes 8388608 | tf_op jit(solution)/shard_map/all_to_all | solution.py:138
  260.1 11.2 %fusion.37 = f32[2,1024,1024]{2,1,0:T(8,128)} fusion(bf16[2,1024,1024]{2,1,0:T(8,128)(2,1)} %bitcast.85, bf16[2,1024,1024]{2,1,0:T(8,128)(2,1)} %all-gather.15.cloned.1.call-done), kind=kOutput, calls=%fused_computation.83 | convolution fusion | flops 4294967296 | bytes 16777216 | tf_op jit(solution)/shard_map/esd,edf->esf/dot_general | solution.py:146
  271.3 6.4 %convolution_convert_fusion = bf16[2,1024,1024]{2,1,0:T(8,128)(2,1)S(1)} fusion(bf16[2,512,1024]{2,1,0:T(8,128)(2,1)} %all-gather.17.cloned.1.call-done, f32[2,1024,1024]{2,1,0:T(8,128)} %fusion.37), kind=kOutput, calls=%fused_computation.18 | convolution fusion | flops 2155872256 | bytes 14680064 | tf_op jit(solution)/shard_map/esf,efd->esd/dot_general | solution.py:148
  277.7 2.5 copy.59
  280.2 7.1 %all-to-all-start.2 = ((bf16[2,16,64,1024]{3,2,0,1:T(8,128)(2,1)}), bf16[2,16,64,1024]{3,2,0,1:T(8,128)(2,1)}, u32[]{:S(2)}, u32[]{:S(2)}) async-start(bf16[2,16,64,1024]{3,2,0,1:T(8,128)(2,1)} %copy.59), calls=%async_computation.2 | async-start | bytes 8388608 | tf_op jit(solution)/shard_map/all_to_all | solution.py:151
  287.4 51.6 %all-to-all-done.2 = bf16[2,16,64,1024]{3,2,0,1:T(8,128)(2,1)} async-done(((bf16[2,16,64,1024]{3,2,0,1:T(8,128)(2,1)}), bf16[2,16,64,1024]{3,2,0,1:T(8,128)(2,1)}, u32[]{:S(2)}, u32[]{:S(2)}) %all-to-all-start.2) | async-done | bytes 4194336 | tf_op jit(solution)/shard_map/all_to_all | solution.py:151
  339.0 8.9 %gather_fusion.1 = bf16[1024,1024]{1,0:T(8,128)(2,1)} fusion(bf16[2048,1024]{1,0:T(8,128)(2,1)} %bitcast.31, s32[1024]{0:T(1024)S(1)} %broadcast_clamp_fusion), kind=kCustom, calls=%fused_computation.1 | custom fusion | bytes 4198400 | tf_op jit(solution)/shard_map/gather | solution.py:159
  348.0 2.3 fusion.10
  (73 shorter events, 8.6 us)
Async XLA Ops:
  6.5 4.4 %copy-start = (bf16[1024,1024]{1,0:T(8,128)(2,1)S(1)}, bf16[1024,1024]{1,0:T(8,128)(2,1)}, u32[]{:S(2)}) copy-start(bf16[1024,1024]{1,0:T(8,128)(2,1)} %param.17) | copy-start | bytes 6291460
  6.5 6.0 %copy-start.9 = (s32[2]{0:T(128)S(1)}, s32[2]{0:T(128)}, u32[]{:S(2)}) copy-start(s32[2]{0:T(128)} %param.21) | copy-start | bytes 28
  6.5 52.1 %copy-start.8 = (s32[2,16]{1,0:T(2,128)S(1)}, s32[2,16]{1,0:T(2,128)}, u32[]{:S(2)}) copy-start(s32[2,16]{1,0:T(2,128)} %param.20) | copy-start | bytes 388
  6.5 51.5 %all-gather.11.cloned.1.call-start = ((), (), s32[]{:S(2)}) async-start(), calls=%async_computation.5 | async-start | bytes 1114112 | tf_op jit(solution)/shard_map/all_gather | solution.py:81
  8.2 99.2 %all-gather.9.cloned.1.call-start = ((), (), s32[]{:S(2)}) async-start(), calls=%async_computation.4 | async-start | bytes 1114112 | tf_op jit(solution)/shard_map/all_gather | solution.py:78
  9.7 142.1 %all-gather.7.cloned.1.call-start = ((), (), s32[]{:S(2)}) async-start(), calls=%async_computation.3 | async-start | bytes 2359296 | tf_op jit(solution)/shard_map/all_gather | solution.py:92
  15.0 173.4 %all-gather.13.cloned.1.call-start = ((), (), s32[]{:S(2)}) async-start(), calls=%async_computation.6 | async-start | bytes 3145728 | tf_op jit(solution)/shard_map/all_gather | solution.py:80
  58.1 202.0 %all-gather.15.cloned.1.call-start = ((), (), s32[]{:S(2)}) async-start(), calls=%async_computation.7 | async-start | bytes 4456448 | tf_op jit(solution)/shard_map/all_gather | solution.py:83
  74.3 2.3 copy-start.4
  109.1 9.3 %copy-start.3 = (bf16[128,1024]{1,0:T(8,128)(2,1)S(1)}, bf16[128,1024]{1,0:T(8,128)(2,1)}, u32[]{:S(2)}) copy-start(bf16[128,1024]{1,0:T(8,128)(2,1)} %param.13) | copy-start | bytes 786436
  109.1 9.3 %copy-start.5 = (f32[1024]{0:T(1024)S(1)}, f32[1024]{0:T(1024)}, u32[]{:S(2)}) copy-start(f32[1024]{0:T(1024)} %param.14) | copy-start | bytes 12292
  120.1 38.6 %copy-start.2 = (bf16[2048,512]{0,1:T(8,128)(2,1)S(1)}, bf16[2048,512]{0,1:T(8,128)(2,1)}, u32[]{:S(2)}) copy-start(bf16[2048,512]{0,1:T(8,128)(2,1)} %get-tuple-element.5) | copy-start | bytes 6291460
  176.8 13.7 %copy-start.6 = (f32[1024]{0:T(1024)S(1)}, f32[1024]{0:T(1024)}, u32[]{:S(2)}) copy-start(f32[1024]{0:T(1024)} %param.15) | copy-start | bytes 12292
  198.6 56.6 %all-to-all-start.1 = ((bf16[16,2,64,1024]{3,2,1,0:T(8,128)(2,1)}), bf16[16,2,64,1024]{3,2,1,0:T(8,128)(2,1)}, u32[]{:S(2)}, u32[]{:S(2)}) async-start(bf16[16,2,64,1024]{3,2,1,0:T(8,128)(2,1)} %bitcast.80), calls=%async_computation.1 | async-start | bytes 8388608 | tf_op jit(solution)/shard_map/all_to_all | solution.py:138
  206.4 64.9 %all-gather.17.cloned.1.call-start = ((), (), s32[]{:S(2)}) async-start(), calls=%async_computation.8 | async-start | bytes 2228224 | tf_op jit(solution)/shard_map/all_gather | solution.py:84
  280.2 7.1 %copy-start.7 = (f32[128,8]{0,1:T(8,128)S(1)}, f32[128,8]{0,1:T(8,128)}, u32[]{:S(2)}) copy-start(f32[128,8]{0,1:T(8,128)} %param.23) | copy-start | bytes 12292
  280.2 58.8 %all-to-all-start.2 = ((bf16[2,16,64,1024]{3,2,0,1:T(8,128)(2,1)}), bf16[2,16,64,1024]{3,2,0,1:T(8,128)(2,1)}, u32[]{:S(2)}, u32[]{:S(2)}) async-start(bf16[2,16,64,1024]{3,2,0,1:T(8,128)(2,1)} %copy.59), calls=%async_computation.2 | async-start | bytes 8388608 | tf_op jit(solution)/shard_map/all_to_all | solution.py:151
  339.0 12.0 %copy-start.1 = (bf16[1024,1024]{1,0:T(8,128)(2,1)S(1)}, bf16[1024,1024]{1,0:T(8,128)(2,1)}, u32[]{:S(2)}) copy-start(bf16[1024,1024]{1,0:T(8,128)(2,1)} %param.17) | copy-start | bytes 6291460
Sparse Core Ops, SparseCore 0:
  9.8 48.2 all-gather.10
  60.5 46.8 all-gather.8
  109.2 42.6 all-gather.6
  153.5 17.7 all-gather.12
  173.0 43.1 all-gather.14
  217.9 38.0 all-gather.16
